TPU v7x, 512 devices: a whole 4x4x16 slice. The times are simulated.
512 devices in a mesh: row: 64 (over x_lo, z, core), col: 8 (over y, x_hi).
Axes of the slice: x: 4 (x_hi: 2, x_lo: 2; x = x_hi * 2 + x_lo), y: 4, z: 16, core: 2. Of those that a mesh axis runs over, the one named last changes fastest.
Arguments:
- features: bfloat16 [128, 131072], P(None, 'row'), may hold values from -6 to 6
- weight_in: bfloat16 [128, 512], P(None, 'col'), may hold values from -0.5 to 0.5
- weight_out: bfloat16 [512, 64], replicated, may hold values from -0.25 to 0.25
- score_grad: bfloat16 [64, 131072], P('col', 'row'), may hold values from -0.011962891 to 0.011962891
- band_blocks: bfloat16 [1024, 3, 128, 128], P('row'), may hold values from -0.25 to 0.25
- long_blocks: bfloat16 [768, 128, 128], P('row'), may hold values from -0.25 to 0.25
- long_rows: int32 [64, 12], P('row'), may hold values from 0 to 15
- long_sources: int32 [64, 12], replicated, may hold values from 0 to 1023, as said below
- long_counts: int32 [64], replicated, may hold values from 1 to 12, as said below
Outputs:
- scores: bfloat16 [64, 131072], P('col', 'row')
- first_grad: float32 [128, 512], P(None, 'col')
- second_grad: float32 [512, 64], P('col')
Inputs may be any that keep to these rules, and one draw needn't show every extreme that they name: `long_sources`: every slot's block column lies on a partition at cycle distance 1 to 3 from the slot's own partition (either direction, indices taken mod the number of partitions); over ALL 12 slots of a partition each of the 6 such partitions is read by exactly 2 slots. Slots s < long_counts[p] are live, the others are ignored; some partition has all 12 live.
All inputs are finite; a program needn't handle non-finite values.
Results may differ from a plain program's by a relative error of at most 0.0065.
Values may be sent and summed in bfloat16 or wider, within the bound.
No kernel may reach another device: no remote copies, remote signals or barrier semaphores. Data moves between devices by JAX's collectives and lax.ppermute only.
A program may use at most 64 MiB of HBM per device.

v0:
```python
import jax
import jax.numpy as jnp
from jax import lax
from jax.sharding import PartitionSpec as P

BLK = 128
NB = 16
REACH = 3
SLOTS = 12


def passed_along(x, axis, by):
    devices = lax.axis_size(axis)
    return lax.ppermute(x, axis, [(i, (i + by) % devices) for i in range(devices)])


def signed_offset(owner_part, partition, row_devices):
    offset = jnp.mod(owner_part - partition, row_devices)
    return jnp.where(offset > row_devices // 2, offset - row_devices, offset)


def slot_table(long_sources, long_counts, partition, row_devices):
    source = lax.dynamic_index_in_dim(long_sources, partition, 0, keepdims=False)
    live_count = lax.dynamic_index_in_dim(long_counts, partition, 0, keepdims=False)
    slot_order = jnp.arange(SLOTS, dtype=jnp.int32)
    is_live = slot_order < live_count
    owner_part = source // NB
    local_block = source - owner_part * NB
    offset = signed_offset(owner_part, partition, row_devices)
    same_offset = (
        (offset[:, None] == offset[None, :])
        & is_live[None, :]
        & (slot_order[None, :] < slot_order[:, None])
    )
    slot_rank = jnp.sum(same_offset.astype(jnp.int32), axis=1)
    return (is_live, offset, local_block, slot_rank)


def distances():
    return [distance for distance in range(-REACH, REACH + 1) if distance != 0]


def aggregate(values, band_blocks, long_blocks, row_ids, long_sources, long_counts):
    feature_rows = values.shape[0]
    row_devices = lax.axis_size("row")
    my_index = lax.axis_index("row")
    blocks = values.reshape(feature_rows, NB, BLK)
    is_live, offset, local_block, slot_rank = slot_table(
        long_sources, long_counts, my_index, row_devices
    )
    position = jnp.where(offset < 0, offset + REACH, offset + REACH - 1)
    received = {}
    for distance in distances():
        arrived = passed_along(values, "row", -distance)
        received[distance] = arrived.reshape(feature_rows, NB, BLK)
    panel_pool = jnp.stack([received[distance] for distance in distances()], 0)
    panel_pool = panel_pool.transpose(0, 2, 1, 3).reshape(2 * REACH * NB, feature_rows, BLK)
    slot_index = position * NB + local_block
    before = received[-1][:, NB - 1]
    beyond = received[1][:, 0]
    slot_index = jnp.clip(slot_index, 0, panel_pool.shape[0] - 1)
    panels = jnp.take(panel_pool, slot_index, axis=0)
    contrib = jnp.einsum("kfm,knm->kfn", panels, long_blocks, preferred_element_type=jnp.float32)
    contrib = contrib * is_live.astype(jnp.float32)[:, None, None]
    targets = (
        (row_ids[:, None] == jnp.arange(NB, dtype=jnp.int32)[None, :]) & is_live[:, None]
    ).astype(jnp.float32)
    far_sum = jnp.einsum("kb,kfn->fbn", targets, contrib, precision=lax.Precision.HIGHEST)
    earlier = jnp.concatenate([before[:, None], blocks[:, :-1]], 1)
    onward = jnp.concatenate([blocks[:, 1:], beyond[:, None]], 1)
    near_sum = jnp.einsum(
        "fbm,bnm->fbn", earlier, band_blocks[:, 0], preferred_element_type=jnp.float32
    )
    near_sum = near_sum + jnp.einsum(
        "fbm,bnm->fbn", blocks, band_blocks[:, 1], preferred_element_type=jnp.float32
    )
    near_sum = near_sum + jnp.einsum(
        "fbm,bnm->fbn", onward, band_blocks[:, 2], preferred_element_type=jnp.float32
    )
    return (near_sum + far_sum).reshape(feature_rows, NB * BLK)


def aggregate_back(values, band_blocks, long_blocks, row_ids, long_sources, long_counts):
    feature_rows = values.shape[0]
    row_devices = lax.axis_size("row")
    my_index = lax.axis_index("row")
    blocks = values.reshape(feature_rows, NB, BLK)
    is_live, offset, local_block, slot_rank = slot_table(
        long_sources, long_counts, my_index, row_devices
    )
    to_prior = jnp.einsum(
        "fbn,bnm->fbm", blocks, band_blocks[:, 0], preferred_element_type=jnp.float32
    )
    middle = jnp.einsum(
        "fbn,bnm->fbm", blocks, band_blocks[:, 1], preferred_element_type=jnp.float32
    )
    to_later = jnp.einsum(
        "fbn,bnm->fbm", blocks, band_blocks[:, 2], preferred_element_type=jnp.float32
    )
    zero_block = jnp.zeros((feature_rows, 1, BLK), jnp.float32)
    summed = (
        middle
        + jnp.concatenate([to_prior[:, 1:], zero_block], 1)
        + jnp.concatenate([zero_block, to_later[:, :-1]], 1)
    )
    edge_prior = to_prior[:, 0]
    edge_later = to_later[:, NB - 1]
    gathered_rows = jnp.take(blocks, row_ids, axis=1)
    contrib = jnp.einsum(
        "fkn,knm->kfm", gathered_rows, long_blocks, preferred_element_type=jnp.float32
    )
    contrib = contrib * is_live.astype(jnp.float32)[:, None, None]
    block_hot = local_block[:, None] == jnp.arange(NB, dtype=jnp.int32)[None, :]
    for distance in distances():
        placing = ((is_live & (offset == distance))[:, None] & block_hot).astype(jnp.float32)
        outgoing = jnp.einsum("kb,kfm->fbm", placing, contrib, precision=lax.Precision.HIGHEST)
        if distance == -1:
            outgoing = outgoing.at[:, NB - 1].add(edge_prior)
        if distance == 1:
            outgoing = outgoing.at[:, 0].add(edge_later)
        summed = summed + passed_along(outgoing, "row", distance)
    return summed.reshape(feature_rows, NB * BLK)


def local(
    features,
    weight_in,
    weight_out,
    score_grad,
    band_blocks,
    long_blocks,
    long_rows,
    long_sources,
    long_counts,
):
    row_ids = long_rows[0]
    hidden_count = weight_in.shape[1]
    class_count = score_grad.shape[0]
    col_index = lax.axis_index("col")
    my_rows = lax.dynamic_slice_in_dim(weight_out, col_index * hidden_count, hidden_count, 0)
    hidden_in = jnp.einsum(
        "ih,in->hn", weight_in, features, preferred_element_type=jnp.float32
    ).astype(jnp.bfloat16)
    hidden_sum = aggregate(hidden_in, band_blocks, long_blocks, row_ids, long_sources, long_counts)
    hidden_act = jax.nn.silu(hidden_sum).astype(jnp.bfloat16)
    out_cols = lax.dynamic_slice_in_dim(weight_out, col_index * class_count, class_count, 1)
    class_sum = jnp.einsum(
        "hc,hn->cn",
        out_cols,
        lax.all_gather(hidden_act, "col", axis=0, tiled=True),
        preferred_element_type=jnp.float32,
    )
    class_in = class_sum.astype(jnp.bfloat16)
    scores = aggregate(
        class_in, band_blocks, long_blocks, row_ids, long_sources, long_counts
    ).astype(jnp.bfloat16)
    class_back = aggregate_back(
        score_grad, band_blocks, long_blocks, row_ids, long_sources, long_counts
    ).astype(jnp.bfloat16)
    shard_piece = lax.all_gather(class_back, "col", axis=0, tiled=True)
    hidden_back = jnp.einsum("hc,cn->hn", my_rows, shard_piece, preferred_element_type=jnp.float32)
    block_grad = jnp.einsum(
        "hn,cn->hc", hidden_act, shard_piece, preferred_element_type=jnp.float32
    )
    second_part = block_grad
    hidden_back, second_part = (hidden_back, second_part)
    sigmoid_val = jax.nn.sigmoid(hidden_sum)
    slope_back = (hidden_back * sigmoid_val * (1.0 + hidden_sum * (1.0 - sigmoid_val))).astype(
        jnp.bfloat16
    )
    input_back = aggregate_back(
        slope_back, band_blocks, long_blocks, row_ids, long_sources, long_counts
    ).astype(jnp.bfloat16)
    first_part = jnp.einsum("in,hn->ih", features, input_back, preferred_element_type=jnp.float32)
    first_grad, second_grad = lax.psum((first_part, second_part), "row")
    return (scores, first_grad, second_grad)


def solution(mesh):
    return jax.shard_map(
        local,
        mesh=mesh,
        in_specs=(
            P(None, "row"),
            P(None, "col"),
            P(),
            P("col", "row"),
            P("row", None, None, None),
            P("row", None, None),
            P("row", None),
            P(),
            P(),
        ),
        out_specs=(P("col", "row"), P(None, "col"), P("col", None)),
        check_vma=False,
    )
```

profile of v0, /device:TPU:2, one launch (start us, length us, event | category | flops | bytes accessed | tf_op | source)
XLA Modules:
  0.0 423.3 jit_solution(10532549555107713151)
XLA Ops:
  15.8 3.3 collective-permute-start.17
  19.3 3.8 collective-permute-start.16
  25.8 3.6 collective-permute-start.15
  31.2 5.8 %collective-permute-start.14 = (f32[8,16,128]{2,0,1:T(8,128)}, f32[8,16,128]{2,0,1:T(8,128)S(1)}, u32[]{:S(2)}, u32[]{:S(2)}) collective-permute-start(f32[8,16,128]{2,0,1:T(8,128)} %fusion.150), channel_id=1, source_target_pairs={{0,504},{8,0},{16,8},{24,16},{32,24},{40,32},{48,40},{56,48},{64,5... | collective-permute-start | bytes 196616 | tf_op jit(solution)/shard_map/ppermute | solution.py:14
  37.3 4.2 collective-permute-start.13
  42.8 3.1 collective-permute-start.12
  46.0 2.9 collective-permute-start
  52.7 5.4 %collective-permute-start.1 = (bf16[64,2048]{1,0:T(8,128)(2,1)S(1)}, bf16[64,2048]{1,0:T(8,128)(2,1)S(1)}, u32[]{:S(2)}, u32[]{:S(2)}) collective-permute-start(bf16[64,2048]{1,0:T(8,128)(2,1)S(1)} %convolution_convert_fusion), channel_id=1, source_target_pairs={{0,504},{8,0},{16,8},{24,16},{32,24},{40,32},{48,40},{56,48},{64,5... | collective-permute-start | bytes 786440 | tf_op jit(solution)/shard_map/ppermute | solution.py:14
  58.1 3.8 collective-permute-start.4
  62.1 41.0 %all_gather.7 = bf16[64,2048]{1,0:T(8,128)(2,1)} all-gather(bf16[8,2048]{1,0:T(8,128)(2,1)S(1)} %fusion.27), channel_id=1, replica_groups=mesh['row'=64,'col'=8] {'col'}, dimensions={0}, use_global_device_ids=true | all-gather | bytes 294912 | tf_op jit(solution)/shard_map/all_gather | solution.py:160
  106.4 6.8 %collective-permute-done.5 = bf16[64,2048]{1,0:T(8,128)(2,1)S(1)} collective-permute-done((bf16[64,2048]{1,0:T(8,128)(2,1)S(1)}, bf16[64,2048]{1,0:T(8,128)(2,1)S(1)}, u32[]{:S(2)}, u32[]{:S(2)}) %collective-permute-start.5) | collective-permute-done | bytes 262176 | tf_op jit(solution)/shard_map/ppermute | solution.py:14
  133.1 2.1 collective-permute-start.21
  137.8 5.5 %collective-permute-start.20 = (f32[64,16,128]{2,0,1:T(8,128)}, f32[64,16,128]{2,0,1:T(8,128)}, u32[]{:S(2)}, u32[]{:S(2)}) collective-permute-start(f32[64,16,128]{2,0,1:T(8,128)} %fusion.105), channel_id=1, source_target_pairs={{0,504},{8,0},{16,8},{24,16},{32,24},{40,32},{48,40},{56,48},{64,5... | collective-permute-start | bytes 1572872 | tf_op jit(solution)/shard_map/ppermute | solution.py:14
  145.8 4.6 %collective-permute-start.19 = (f32[64,16,128]{2,0,1:T(8,128)}, f32[64,16,128]{2,0,1:T(8,128)}, u32[]{:S(2)}, u32[]{:S(2)}) collective-permute-start(f32[64,16,128]{2,0,1:T(8,128)} %bitcast.315), channel_id=1, source_target_pairs={{0,496},{8,504},{16,0},{24,8},{32,16},{40,24},{48,32},{56,40},{64,... | collective-permute-start | bytes 1572872 | tf_op jit(solution)/shard_map/ppermute | solution.py:14
  151.4 3.3 collective-permute-start.18
  155.9 5.4 %collective-permute-done.22 = f32[64,16,128]{2,0,1:T(8,128)} collective-permute-done((f32[64,16,128]{2,0,1:T(8,128)}, f32[64,16,128]{2,0,1:T(8,128)}, u32[]{:S(2)}, u32[]{:S(2)}) %collective-permute-start.22) | collective-permute-done | bytes 524320 | tf_op jit(solution)/shard_map/ppermute | solution.py:14
  161.2 2.5 collective-permute-done.21
  163.7 14.8 %collective-permute-done.18 = f32[64,16,128]{2,0,1:T(8,128)} collective-permute-done((f32[64,16,128]{2,0,1:T(8,128)}, f32[64,16,128]{2,0,1:T(8,128)}, u32[]{:S(2)}, u32[]{:S(2)}) %collective-permute-start.18) | collective-permute-done | bytes 524320 | tf_op jit(solution)/shard_map/ppermute | solution.py:14
  178.5 2.2 fusion.14
  181.0 209.5 %all-reduce.4 = (f32[128,64]{0,1:T(8,128)}, f32[64,64]{1,0:T(8,128)}) all-reduce(f32[128,64]{0,1:T(8,128)S(1)} %convolution_bitcast_fusion.6, f32[64,64]{1,0:T(8,128)S(1)} %fusion.208), channel_id=1, replica_groups=mesh['row'=64,'col'=8] {'row'}, use_global_device_ids=true, to_apply=%region_0.1 | all-reduce | flops 12288 | bytes 98304 | tf_op jit(solution)/shard_map/psum | solution.py:175
  398.7 5.8 %collective-permute-start.7 = (bf16[8,2048]{1,0:T(8,128)(2,1)S(1)}, bf16[8,2048]{1,0:T(8,128)(2,1)S(1)}, u32[]{:S(2)}, u32[]{:S(2)}) collective-permute-start(bf16[8,2048]{1,0:T(8,128)(2,1)S(1)} %convolution_convert_fusion.1), channel_id=1, source_target_pairs={{0,504},{8,0},{16,8},{24,16},{32,24},{40,32},{48,40},{56,48},{64,5... | collective-permute-start | bytes 98312 | tf_op jit(solution)/shard_map/ppermute | solution.py:14
  404.5 3.6 collective-permute-start.10
  408.2 3.5 collective-permute-start.11
  411.8 2.2 collective-permute-done.11
  (189 shorter events, 59.5 us)
Async XLA Ops:
  7.2 383.3 %all-gather.2.cloned.1.call-start = ((), (), s32[]{:S(2)}) async-start(), calls=%async_computation | async-start | bytes 2359296 | tf_op jit(solution)/shard_map/all_gather | solution.py:150
  15.8 27.1 %collective-permute-start.17 = (f32[8,16,128]{2,0,1:T(8,128)S(1)}, f32[8,16,128]{2,0,1:T(8,128)S(1)}, u32[]{:S(2)}, u32[]{:S(2)}) collective-permute-start(f32[8,16,128]{2,0,1:T(8,128)S(1)} %bitcast.346), channel_id=1, source_target_pairs={{0,24},{8,32},{16,40},{24,48},{32,56},{40,64},{48,72},{56,80},{64,... | collective-permute-start | bytes 196616 | tf_op jit(solution)/shard_map/ppermute | solution.py:14
  19.3 26.7 %collective-permute-start.16 = (f32[8,16,128]{2,0,1:T(8,128)S(1)}, f32[8,16,128]{2,0,1:T(8,128)S(1)}, u32[]{:S(2)}, u32[]{:S(2)}) collective-permute-start(f32[8,16,128]{2,0,1:T(8,128)S(1)} %bitcast.345), channel_id=1, source_target_pairs={{0,16},{8,24},{16,32},{24,40},{32,48},{40,56},{48,64},{56,72},{64,... | collective-permute-start | bytes 196616 | tf_op jit(solution)/shard_map/ppermute | solution.py:14
  25.8 23.0 %collective-permute-start.15 = (f32[8,16,128]{2,0,1:T(8,128)}, f32[8,16,128]{2,0,1:T(8,128)S(1)}, u32[]{:S(2)}, u32[]{:S(2)}) collective-permute-start(f32[8,16,128]{2,0,1:T(8,128)} %fusion.149), channel_id=1, source_target_pairs={{0,8},{8,16},{16,24},{24,32},{32,40},{40,48},{48,56},{56,64},{64,7... | collective-permute-start | bytes 196616 | tf_op jit(solution)/shard_map/ppermute | solution.py:14
  31.2 19.6 %collective-permute-start.14 = (f32[8,16,128]{2,0,1:T(8,128)}, f32[8,16,128]{2,0,1:T(8,128)S(1)}, u32[]{:S(2)}, u32[]{:S(2)}) collective-permute-start(f32[8,16,128]{2,0,1:T(8,128)} %fusion.150), channel_id=1, source_target_pairs={{0,504},{8,0},{16,8},{24,16},{32,24},{40,32},{48,40},{56,48},{64,5... | collective-permute-start | bytes 196616 | tf_op jit(solution)/shard_map/ppermute | solution.py:14
  37.3 15.5 %collective-permute-start.13 = (f32[8,16,128]{2,0,1:T(8,128)S(1)}, f32[8,16,128]{2,0,1:T(8,128)S(1)}, u32[]{:S(2)}, u32[]{:S(2)}) collective-permute-start(f32[8,16,128]{2,0,1:T(8,128)S(1)} %bitcast.347), channel_id=1, source_target_pairs={{0,496},{8,504},{16,0},{24,8},{32,16},{40,24},{48,32},{56,40},{64,... | collective-permute-start | bytes 196616 | tf_op jit(solution)/shard_map/ppermute | solution.py:14
  42.8 15.3 %collective-permute-start.12 = (f32[8,16,128]{2,0,1:T(8,128)S(1)}, f32[8,16,128]{2,0,1:T(8,128)S(1)}, u32[]{:S(2)}, u32[]{:S(2)}) collective-permute-start(f32[8,16,128]{2,0,1:T(8,128)S(1)} %bitcast.348), channel_id=1, source_target_pairs={{0,488},{8,496},{16,504},{24,0},{32,8},{40,16},{48,24},{56,32},{64... | collective-permute-start | bytes 196616 | tf_op jit(solution)/shard_map/ppermute | solution.py:14
  46.0 57.2 %collective-permute-start = (bf16[64,2048]{1,0:T(8,128)(2,1)S(1)}, bf16[64,2048]{1,0:T(8,128)(2,1)S(1)}, u32[]{:S(2)}, u32[]{:S(2)}) collective-permute-start(bf16[64,2048]{1,0:T(8,128)(2,1)S(1)} %convolution_convert_fusion), channel_id=1, source_target_pairs={{0,8},{8,16},{16,24},{24,32},{32,40},{40,48},{48,56},{56,64},{64,7... | collective-permute-start | bytes 786440 | tf_op jit(solution)/shard_map/ppermute | solution.py:14
  48.8 56.3 %collective-permute-start.2 = (bf16[64,2048]{1,0:T(8,128)(2,1)S(1)}, bf16[64,2048]{1,0:T(8,128)(2,1)S(1)}, u32[]{:S(2)}, u32[]{:S(2)}) collective-permute-start(bf16[64,2048]{1,0:T(8,128)(2,1)S(1)} %convolution_convert_fusion), channel_id=1, source_target_pairs={{0,24},{8,32},{16,40},{24,48},{32,56},{40,64},{48,72},{56,80},{64,... | collective-permute-start | bytes 786440 | tf_op jit(solution)/shard_map/ppermute | solution.py:14
  50.8 54.4 %collective-permute-start.3 = (bf16[64,2048]{1,0:T(8,128)(2,1)S(1)}, bf16[64,2048]{1,0:T(8,128)(2,1)S(1)}, u32[]{:S(2)}, u32[]{:S(2)}) collective-permute-start(bf16[64,2048]{1,0:T(8,128)(2,1)S(1)} %convolution_convert_fusion), channel_id=1, source_target_pairs={{0,16},{8,24},{16,32},{24,40},{32,48},{40,56},{48,64},{56,72},{64,... | collective-permute-start | bytes 786440 | tf_op jit(solution)/shard_map/ppermute | solution.py:14
  52.7 52.5 %collective-permute-start.1 = (bf16[64,2048]{1,0:T(8,128)(2,1)S(1)}, bf16[64,2048]{1,0:T(8,128)(2,1)S(1)}, u32[]{:S(2)}, u32[]{:S(2)}) collective-permute-start(bf16[64,2048]{1,0:T(8,128)(2,1)S(1)} %convolution_convert_fusion), channel_id=1, source_target_pairs={{0,504},{8,0},{16,8},{24,16},{32,24},{40,32},{48,40},{56,48},{64,5... | collective-permute-start | bytes 786440 | tf_op jit(solution)/shard_map/ppermute | solution.py:14
  58.1 47.3 %collective-permute-start.4 = (bf16[64,2048]{1,0:T(8,128)(2,1)S(1)}, bf16[64,2048]{1,0:T(8,128)(2,1)S(1)}, u32[]{:S(2)}, u32[]{:S(2)}) collective-permute-start(bf16[64,2048]{1,0:T(8,128)(2,1)S(1)} %convolution_convert_fusion), channel_id=1, source_target_pairs={{0,496},{8,504},{16,0},{24,8},{32,16},{40,24},{48,32},{56,40},{64,... | collective-permute-start | bytes 786440 | tf_op jit(solution)/shard_map/ppermute | solution.py:14
  103.1 10.0 %collective-permute-start.5 = (bf16[64,2048]{1,0:T(8,128)(2,1)S(1)}, bf16[64,2048]{1,0:T(8,128)(2,1)S(1)}, u32[]{:S(2)}, u32[]{:S(2)}) collective-permute-start(bf16[64,2048]{1,0:T(8,128)(2,1)S(1)} %convolution_convert_fusion), channel_id=1, source_target_pairs={{0,488},{8,496},{16,504},{24,0},{32,8},{40,16},{48,24},{56,32},{64... | collective-permute-start | bytes 786440 | tf_op jit(solution)/shard_map/ppermute | solution.py:14
  124.9 26.5 %collective-permute-start.23 = (f32[64,16,128]{2,0,1:T(8,128)S(1)}, f32[64,16,128]{2,0,1:T(8,128)}, u32[]{:S(2)}, u32[]{:S(2)}) collective-permute-start(f32[64,16,128]{2,0,1:T(8,128)S(1)} %bitcast.333), channel_id=1, source_target_pairs={{0,24},{8,32},{16,40},{24,48},{32,56},{40,64},{48,72},{56,80},{64,... | collective-permute-start | bytes 1572872 | tf_op jit(solution)/shard_map/ppermute | solution.py:14
  128.5 32.7 %collective-permute-start.22 = (f32[64,16,128]{2,0,1:T(8,128)}, f32[64,16,128]{2,0,1:T(8,128)}, u32[]{:S(2)}, u32[]{:S(2)}) collective-permute-start(f32[64,16,128]{2,0,1:T(8,128)} %bitcast.314), channel_id=1, source_target_pairs={{0,16},{8,24},{16,32},{24,40},{32,48},{40,56},{48,64},{56,72},{64,... | collective-permute-start | bytes 1572872 | tf_op jit(solution)/shard_map/ppermute | solution.py:14
  133.1 30.6 %collective-permute-start.21 = (f32[64,16,128]{2,0,1:T(8,128)}, f32[64,16,128]{2,0,1:T(8,128)}, u32[]{:S(2)}, u32[]{:S(2)}) collective-permute-start(f32[64,16,128]{2,0,1:T(8,128)} %fusion.104), channel_id=1, source_target_pairs={{0,8},{8,16},{16,24},{24,32},{32,40},{40,48},{48,56},{56,64},{64,7... | collective-permute-start | bytes 1572872 | tf_op jit(solution)/shard_map/ppermute | solution.py:14
  137.8 25.9 %collective-permute-start.20 = (f32[64,16,128]{2,0,1:T(8,128)}, f32[64,16,128]{2,0,1:T(8,128)}, u32[]{:S(2)}, u32[]{:S(2)}) collective-permute-start(f32[64,16,128]{2,0,1:T(8,128)} %fusion.105), channel_id=1, source_target_pairs={{0,504},{8,0},{16,8},{24,16},{32,24},{40,32},{48,40},{56,48},{64,5... | collective-permute-start | bytes 1572872 | tf_op jit(solution)/shard_map/ppermute | solution.py:14
  145.8 17.9 %collective-permute-start.19 = (f32[64,16,128]{2,0,1:T(8,128)}, f32[64,16,128]{2,0,1:T(8,128)}, u32[]{:S(2)}, u32[]{:S(2)}) collective-permute-start(f32[64,16,128]{2,0,1:T(8,128)} %bitcast.315), channel_id=1, source_target_pairs={{0,496},{8,504},{16,0},{24,8},{32,16},{40,24},{48,32},{56,40},{64,... | collective-permute-start | bytes 1572872 | tf_op jit(solution)/shard_map/ppermute | solution.py:14
  151.4 27.1 %collective-permute-start.18 = (f32[64,16,128]{2,0,1:T(8,128)}, f32[64,16,128]{2,0,1:T(8,128)}, u32[]{:S(2)}, u32[]{:S(2)}) collective-permute-start(f32[64,16,128]{2,0,1:T(8,128)} %bitcast.316), channel_id=1, source_target_pairs={{0,488},{8,496},{16,504},{24,0},{32,8},{40,16},{48,24},{56,32},{64... | collective-permute-start | bytes 1572872 | tf_op jit(solution)/shard_map/ppermute | solution.py:14
  392.9 18.8 %collective-permute-start.6 = (bf16[8,2048]{1,0:T(8,128)(2,1)S(1)}, bf16[8,2048]{1,0:T(8,128)(2,1)S(1)}, u32[]{:S(2)}, u32[]{:S(2)}) collective-permute-start(bf16[8,2048]{1,0:T(8,128)(2,1)S(1)} %convolution_convert_fusion.1), channel_id=1, source_target_pairs={{0,8},{8,16},{16,24},{24,32},{32,40},{40,48},{48,56},{56,64},{64,7... | collective-permute-start | bytes 98312 | tf_op jit(solution)/shard_map/ppermute | solution.py:14
  394.9 13.3 %collective-permute-start.8 = (bf16[8,2048]{1,0:T(8,128)(2,1)S(1)}, bf16[8,2048]{1,0:T(8,128)(2,1)S(1)}, u32[]{:S(2)}, u32[]{:S(2)}) collective-permute-start(bf16[8,2048]{1,0:T(8,128)(2,1)S(1)} %convolution_convert_fusion.1), channel_id=1, source_target_pairs={{0,24},{8,32},{16,40},{24,48},{32,56},{40,64},{48,72},{56,80},{64,... | collective-permute-start | bytes 98312 | tf_op jit(solution)/shard_map/ppermute | solution.py:14
  396.8 14.9 %collective-permute-start.9 = (bf16[8,2048]{1,0:T(8,128)(2,1)S(1)}, bf16[8,2048]{1,0:T(8,128)(2,1)S(1)}, u32[]{:S(2)}, u32[]{:S(2)}) collective-permute-start(bf16[8,2048]{1,0:T(8,128)(2,1)S(1)} %convolution_convert_fusion.1), channel_id=1, source_target_pairs={{0,16},{8,24},{16,32},{24,40},{32,48},{40,56},{48,64},{56,72},{64,... | collective-permute-start | bytes 98312 | tf_op jit(solution)/shard_map/ppermute | solution.py:14
  398.7 13.0 %collective-permute-start.7 = (bf16[8,2048]{1,0:T(8,128)(2,1)S(1)}, bf16[8,2048]{1,0:T(8,128)(2,1)S(1)}, u32[]{:S(2)}, u32[]{:S(2)}) collective-permute-start(bf16[8,2048]{1,0:T(8,128)(2,1)S(1)} %convolution_convert_fusion.1), channel_id=1, source_target_pairs={{0,504},{8,0},{16,8},{24,16},{32,24},{40,32},{48,40},{56,48},{64,5... | collective-permute-start | bytes 98312 | tf_op jit(solution)/shard_map/ppermute | solution.py:14
  404.5 7.3 %collective-permute-start.10 = (bf16[8,2048]{1,0:T(8,128)(2,1)S(1)}, bf16[8,2048]{1,0:T(8,128)(2,1)S(1)}, u32[]{:S(2)}, u32[]{:S(2)}) collective-permute-start(bf16[8,2048]{1,0:T(8,128)(2,1)S(1)} %convolution_convert_fusion.1), channel_id=1, source_target_pairs={{0,496},{8,504},{16,0},{24,8},{32,16},{40,24},{48,32},{56,40},{64,... | collective-permute-start | bytes 98312 | tf_op jit(solution)/shard_map/ppermute | solution.py:14
  (32 other events, 660.2 us)
Sparse Core Ops, SparseCore 0:
  121.1 77.6 all-gather.1
where the time goes:
time: 425 us; the launch traced here: 423 us
  blocking collectives  251 us (59%)
  starting transfers between devices  79.6 us (19%)
  waiting for transfers between devices  31.7 us (7%)
  matrix products  21.6 us (5%)
  local copies, waits for them, and re-layouts  18 us (4%)
  between operations  15.3 us (4%)
  other arithmetic  6.68 us (2%)
    psum x1, blocking collectives, local(): first_grad, second_grad = lax.psum((first_part, second_part), 'row')  210 us
    ppermute x24, starting transfers between devices, passed_along(): lax.ppermute(x, axis, [(i, (i + by) % devices) for i in range(devices)])  79.6 us
    all_gather x1, blocking collectives, local(): shard_piece = lax.all_gather(class_back, 'col', axis=0, tiled=True)  41 us
    ppermute x24, waiting for transfers between devices, passed_along(): lax.ppermute(x, axis, [(i, (i + by) % devices) for i in range(devices)])  31.7 us
  transfers between devices with their start and end apart: 25, of which 5 were waited for; matrix products, arithmetic and copies ran while one was open for 6% of the time, Pallas kernels for 0%

commit v1 on v0

--- a/solution.py
+++ b/solution.py
@@ -157,7 +157,10 @@
     class_back = aggregate_back(
         score_grad, band_blocks, long_blocks, row_ids, long_sources, long_counts
     ).astype(jnp.bfloat16)
-    shard_piece = lax.all_gather(class_back, "col", axis=0, tiled=True)
+    k_now = lax.psum(1, axis_name="col")
+    odd = jnp.stack([class_back] * k_now)
+    tmp = lax.all_to_all(odd, axis_name="col", split_axis=0, concat_axis=0)
+    shard_piece = jnp.concatenate(tmp, 0)
     hidden_back = jnp.einsum("hc,cn->hn", my_rows, shard_piece, preferred_element_type=jnp.float32)
     block_grad = jnp.einsum(
         "hn,cn->hc", hidden_act, shard_piece, preferred_element_type=jnp.float32

time: 425 us -> 396 us (0.932)
  the two profiles are of different devices: /device:TPU:2 before, /device:TPU:1 now
where the time goes in v1:
time: 396 us; the launch traced here: 395 us
  blocking collectives  203 us (51%)
  starting transfers between devices  98.7 us (25%)
  local copies, waits for them, and re-layouts  24.5 us (6%)
  matrix products  22.8 us (6%)
  waiting for transfers between devices  22.2 us (6%)
  between operations  15.2 us (4%)
  other arithmetic  7.74 us (2%)
    psum x1, blocking collectives, local(): first_grad, second_grad = lax.psum((first_part, second_part), 'row')  203 us
    ppermute x24, starting transfers between devices, passed_along(): lax.ppermute(x, axis, [(i, (i + by) % devices) for i in range(devices)])  92.3 us
    ppermute x24, waiting for transfers between devices, passed_along(): lax.ppermute(x, axis, [(i, (i + by) % devices) for i in range(devices)])  22.1 us
    unnamed x84, local copies, waits for them, and re-layouts  8.34 us
  transfers between devices with their start and end apart: 26, of which 5 were waited for; matrix products, arithmetic and copies ran while one was open for 12% of the time, Pallas kernels for 0%

profile of v1, /device:TPU:1, one launch (start us, length us, event | category | flops | bytes accessed | tf_op | source)
XLA Modules:
  0.0 394.5 jit_solution(14340643697248574760)
XLA Ops:
  9.2 6.3 %collective-permute-start.2 = (bf16[64,2048]{1,0:T(8,128)(2,1)S(1)}, bf16[64,2048]{1,0:T(8,128)(2,1)S(1)}, u32[]{:S(2)}, u32[]{:S(2)}) collective-permute-start(bf16[64,2048]{1,0:T(8,128)(2,1)S(1)} %convolution_convert_fusion), channel_id=1, source_target_pairs={{0,24},{8,32},{16,40},{24,48},{32,56},{40,64},{48,72},{56,80},{64,... | collective-permute-start | bytes 786440 | tf_op jit(solution)/shard_map/ppermute | solution.py:14
  25.7 4.4 %collective-permute-start.14 = (f32[8,16,128]{2,0,1:T(8,128)S(1)}, f32[8,16,128]{2,0,1:T(8,128)S(1)}, u32[]{:S(2)}, u32[]{:S(2)}) collective-permute-start(f32[8,16,128]{2,0,1:T(8,128)S(1)} %fusion.155), channel_id=1, source_target_pairs={{0,504},{8,0},{16,8},{24,16},{32,24},{40,32},{48,40},{56,48},{64,5... | collective-permute-start | bytes 196616 | tf_op jit(solution)/shard_map/ppermute | solution.py:14
  30.6 1.9 collective-permute-start.15
  32.7 9.8 %collective-permute-start.13 = (f32[8,16,128]{2,0,1:T(8,128)S(1)}, f32[8,16,128]{2,0,1:T(8,128)}, u32[]{:S(2)}, u32[]{:S(2)}) collective-permute-start(f32[8,16,128]{2,0,1:T(8,128)S(1)} %bitcast.352), channel_id=1, source_target_pairs={{0,496},{8,504},{16,0},{24,8},{32,16},{40,24},{48,32},{56,40},{64,... | collective-permute-start | bytes 196616 | tf_op jit(solution)/shard_map/ppermute | solution.py:14
  42.9 1.9 collective-permute-start.16
  48.5 5.8 %collective-permute-start.12 = (f32[8,16,128]{2,0,1:T(8,128)}, f32[8,16,128]{2,0,1:T(8,128)}, u32[]{:S(2)}, u32[]{:S(2)}) collective-permute-start(f32[8,16,128]{2,0,1:T(8,128)} %bitcast.331), channel_id=1, source_target_pairs={{0,488},{8,496},{16,504},{24,0},{32,8},{40,16},{48,24},{56,32},{64... | collective-permute-start | bytes 196616 | tf_op jit(solution)/shard_map/ppermute | solution.py:14
  55.1 1.9 collective-permute-start.3
  57.0 3.1 collective-permute-start
  60.1 2.3 collective-permute-start.1
  62.5 5.4 %collective-permute-start.4 = (bf16[64,2048]{1,0:T(8,128)(2,1)S(1)}, bf16[64,2048]{1,0:T(8,128)(2,1)}, u32[]{:S(2)}, u32[]{:S(2)}) collective-permute-start(bf16[64,2048]{1,0:T(8,128)(2,1)S(1)} %convolution_convert_fusion), channel_id=1, source_target_pairs={{0,496},{8,504},{16,0},{24,8},{32,16},{40,24},{48,32},{56,40},{64,... | collective-permute-start | bytes 786440 | tf_op jit(solution)/shard_map/ppermute | solution.py:14
  73.0 6.4 %all-to-all-start = ((bf16[8,8,2048]{2,1,0:T(8,128)(2,1)}), bf16[8,8,2048]{2,1,0:T(8,128)(2,1)}, u32[]{:S(2)}, u32[]{:S(2)}) async-start(bf16[8,8,2048]{2,1,0:T(8,128)(2,1)} %stack.8), calls=%async_computation | async-start | bytes 524288 | tf_op jit(solution)/shard_map/all_to_all | solution.py:162
  86.6 2.1 gather_fusion
  97.6 3.8 collective-permute-start.20
  108.3 7.5 %collective-permute-start.19 = (f32[64,16,128]{2,0,1:T(8,128)}, f32[64,16,128]{2,0,1:T(8,128)}, u32[]{:S(2)}, u32[]{:S(2)}) collective-permute-start(f32[64,16,128]{2,0,1:T(8,128)} %bitcast.325), channel_id=1, source_target_pairs={{0,496},{8,504},{16,0},{24,8},{32,16},{40,24},{48,32},{56,40},{64,... | collective-permute-start | bytes 1572872 | tf_op jit(solution)/shard_map/ppermute | solution.py:14
  121.1 6.1 %collective-permute-start.18 = (f32[64,16,128]{2,0,1:T(8,128)}, f32[64,16,128]{2,0,1:T(8,128)}, u32[]{:S(2)}, u32[]{:S(2)}) collective-permute-start(f32[64,16,128]{2,0,1:T(8,128)} %bitcast.326), channel_id=1, source_target_pairs={{0,488},{8,496},{16,504},{24,0},{32,8},{40,16},{48,24},{56,32},{64... | collective-permute-start | bytes 1572872 | tf_op jit(solution)/shard_map/ppermute | solution.py:14
  134.4 10.3 %collective-permute-done.18 = f32[64,16,128]{2,0,1:T(8,128)} collective-permute-done((f32[64,16,128]{2,0,1:T(8,128)}, f32[64,16,128]{2,0,1:T(8,128)}, u32[]{:S(2)}, u32[]{:S(2)}) %collective-permute-start.18) | collective-permute-done | bytes 524320 | tf_op jit(solution)/shard_map/ppermute | solution.py:14
  144.7 7.5 %collective-permute-done.23 = f32[64,16,128]{2,0,1:T(8,128)} collective-permute-done((f32[64,16,128]{2,0,1:T(8,128)}, f32[64,16,128]{2,0,1:T(8,128)}, u32[]{:S(2)}, u32[]{:S(2)}) %collective-permute-start.23) | collective-permute-done | bytes 524320 | tf_op jit(solution)/shard_map/ppermute | solution.py:14
  152.3 2.2 fusion.13
  154.8 203.4 %all-reduce.4 = (f32[128,64]{0,1:T(8,128)}, f32[64,64]{1,0:T(8,128)}) all-reduce(f32[128,64]{0,1:T(8,128)S(1)} %convolution_bitcast_fusion.6, f32[64,64]{1,0:T(8,128)S(1)} %fusion.74), channel_id=1, replica_groups=mesh['row'=64,'col'=8] {'row'}, use_global_device_ids=true, to_apply=%region_0.1 | all-reduce | flops 12288 | bytes 98304 | tf_op jit(solution)/shard_map/psum | solution.py:178
  358.3 2.0 convolution_convert_fusion.1
  364.1 3.6 collective-permute-start.6
  367.7 4.7 %collective-permute-start.7 = (bf16[8,2048]{1,0:T(8,128)(2,1)S(1)}, bf16[8,2048]{1,0:T(8,128)(2,1)S(1)}, u32[]{:S(2)}, u32[]{:S(2)}) collective-permute-start(bf16[8,2048]{1,0:T(8,128)(2,1)S(1)} %convolution_convert_fusion.1), channel_id=1, source_target_pairs={{0,504},{8,0},{16,8},{24,16},{32,24},{40,32},{48,40},{56,48},{64,5... | collective-permute-start | bytes 98312 | tf_op jit(solution)/shard_map/ppermute | solution.py:14
  372.4 5.8 %collective-permute-start.10 = (bf16[8,2048]{1,0:T(8,128)(2,1)S(1)}, bf16[8,2048]{1,0:T(8,128)(2,1)S(1)}, u32[]{:S(2)}, u32[]{:S(2)}) collective-permute-start(bf16[8,2048]{1,0:T(8,128)(2,1)S(1)} %convolution_convert_fusion.1), channel_id=1, source_target_pairs={{0,496},{8,504},{16,0},{24,8},{32,16},{40,24},{48,32},{56,40},{64,... | collective-permute-start | bytes 98312 | tf_op jit(solution)/shard_map/ppermute | solution.py:14
  378.5 4.7 %collective-permute-start.11 = (bf16[8,2048]{1,0:T(8,128)(2,1)S(1)}, bf16[8,2048]{1,0:T(8,128)(2,1)S(1)}, u32[]{:S(2)}, u32[]{:S(2)}) collective-permute-start(bf16[8,2048]{1,0:T(8,128)(2,1)S(1)} %convolution_convert_fusion.1), channel_id=1, source_target_pairs={{0,488},{8,496},{16,504},{24,0},{32,8},{40,16},{48,24},{56,32},{64... | collective-permute-start | bytes 98312 | tf_op jit(solution)/shard_map/ppermute | solution.py:14
  (195 shorter events, 66.4 us)
Async XLA Ops:
  9.2 59.9 %collective-permute-start.2 = (bf16[64,2048]{1,0:T(8,128)(2,1)S(1)}, bf16[64,2048]{1,0:T(8,128)(2,1)S(1)}, u32[]{:S(2)}, u32[]{:S(2)}) collective-permute-start(bf16[64,2048]{1,0:T(8,128)(2,1)S(1)} %convolution_convert_fusion), channel_id=1, source_target_pairs={{0,24},{8,32},{16,40},{24,48},{32,56},{40,64},{48,72},{56,80},{64,... | collective-permute-start | bytes 786440 | tf_op jit(solution)/shard_map/ppermute | solution.py:14
  25.7 20.8 %collective-permute-start.14 = (f32[8,16,128]{2,0,1:T(8,128)S(1)}, f32[8,16,128]{2,0,1:T(8,128)S(1)}, u32[]{:S(2)}, u32[]{:S(2)}) collective-permute-start(f32[8,16,128]{2,0,1:T(8,128)S(1)} %fusion.155), channel_id=1, source_target_pairs={{0,504},{8,0},{16,8},{24,16},{32,24},{40,32},{48,40},{56,48},{64,5... | collective-permute-start | bytes 196616 | tf_op jit(solution)/shard_map/ppermute | solution.py:14
  30.6 17.8 %collective-permute-start.15 = (f32[8,16,128]{2,0,1:T(8,128)S(1)}, f32[8,16,128]{2,0,1:T(8,128)S(1)}, u32[]{:S(2)}, u32[]{:S(2)}) collective-permute-start(f32[8,16,128]{2,0,1:T(8,128)S(1)} %fusion.154), channel_id=1, source_target_pairs={{0,8},{8,16},{16,24},{24,32},{32,40},{40,48},{48,56},{56,64},{64,7... | collective-permute-start | bytes 196616 | tf_op jit(solution)/shard_map/ppermute | solution.py:14
  32.7 22.3 %collective-permute-start.13 = (f32[8,16,128]{2,0,1:T(8,128)S(1)}, f32[8,16,128]{2,0,1:T(8,128)}, u32[]{:S(2)}, u32[]{:S(2)}) collective-permute-start(f32[8,16,128]{2,0,1:T(8,128)S(1)} %bitcast.352), channel_id=1, source_target_pairs={{0,496},{8,504},{16,0},{24,8},{32,16},{40,24},{48,32},{56,40},{64,... | collective-permute-start | bytes 196616 | tf_op jit(solution)/shard_map/ppermute | solution.py:14
  42.9 14.2 %collective-permute-start.16 = (f32[8,16,128]{2,0,1:T(8,128)S(1)}, f32[8,16,128]{2,0,1:T(8,128)}, u32[]{:S(2)}, u32[]{:S(2)}) collective-permute-start(f32[8,16,128]{2,0,1:T(8,128)S(1)} %bitcast.351), channel_id=1, source_target_pairs={{0,16},{8,24},{16,32},{24,40},{32,48},{40,56},{48,64},{56,72},{64,... | collective-permute-start | bytes 196616 | tf_op jit(solution)/shard_map/ppermute | solution.py:14
  46.5 13.6 %collective-permute-start.17 = (f32[8,16,128]{2,0,1:T(8,128)}, f32[8,16,128]{2,0,1:T(8,128)}, u32[]{:S(2)}, u32[]{:S(2)}) collective-permute-start(f32[8,16,128]{2,0,1:T(8,128)} %bitcast.328), channel_id=1, source_target_pairs={{0,24},{8,32},{16,40},{24,48},{32,56},{40,64},{48,72},{56,80},{64,... | collective-permute-start | bytes 196616 | tf_op jit(solution)/shard_map/ppermute | solution.py:14
  48.5 14.0 %collective-permute-start.12 = (f32[8,16,128]{2,0,1:T(8,128)}, f32[8,16,128]{2,0,1:T(8,128)}, u32[]{:S(2)}, u32[]{:S(2)}) collective-permute-start(f32[8,16,128]{2,0,1:T(8,128)} %bitcast.331), channel_id=1, source_target_pairs={{0,488},{8,496},{16,504},{24,0},{32,8},{40,16},{48,24},{56,32},{64... | collective-permute-start | bytes 196616 | tf_op jit(solution)/shard_map/ppermute | solution.py:14
  55.1 24.3 %collective-permute-start.3 = (bf16[64,2048]{1,0:T(8,128)(2,1)S(1)}, bf16[64,2048]{1,0:T(8,128)(2,1)S(1)}, u32[]{:S(2)}, u32[]{:S(2)}) collective-permute-start(bf16[64,2048]{1,0:T(8,128)(2,1)S(1)} %convolution_convert_fusion), channel_id=1, source_target_pairs={{0,16},{8,24},{16,32},{24,40},{32,48},{40,56},{48,64},{56,72},{64,... | collective-permute-start | bytes 786440 | tf_op jit(solution)/shard_map/ppermute | solution.py:14
  57.0 22.4 %collective-permute-start = (bf16[64,2048]{1,0:T(8,128)(2,1)S(1)}, bf16[64,2048]{1,0:T(8,128)(2,1)S(1)}, u32[]{:S(2)}, u32[]{:S(2)}) collective-permute-start(bf16[64,2048]{1,0:T(8,128)(2,1)S(1)} %convolution_convert_fusion), channel_id=1, source_target_pairs={{0,8},{8,16},{16,24},{24,32},{32,40},{40,48},{48,56},{56,64},{64,7... | collective-permute-start | bytes 786440 | tf_op jit(solution)/shard_map/ppermute | solution.py:14
  60.1 19.4 %collective-permute-start.1 = (bf16[64,2048]{1,0:T(8,128)(2,1)S(1)}, bf16[64,2048]{1,0:T(8,128)(2,1)}, u32[]{:S(2)}, u32[]{:S(2)}) collective-permute-start(bf16[64,2048]{1,0:T(8,128)(2,1)S(1)} %convolution_convert_fusion), channel_id=1, source_target_pairs={{0,504},{8,0},{16,8},{24,16},{32,24},{40,32},{48,40},{56,48},{64,5... | collective-permute-start | bytes 786440 | tf_op jit(solution)/shard_map/ppermute | solution.py:14
  62.5 18.1 %collective-permute-start.4 = (bf16[64,2048]{1,0:T(8,128)(2,1)S(1)}, bf16[64,2048]{1,0:T(8,128)(2,1)}, u32[]{:S(2)}, u32[]{:S(2)}) collective-permute-start(bf16[64,2048]{1,0:T(8,128)(2,1)S(1)} %convolution_convert_fusion), channel_id=1, source_target_pairs={{0,496},{8,504},{16,0},{24,8},{32,16},{40,24},{48,32},{56,40},{64,... | collective-permute-start | bytes 786440 | tf_op jit(solution)/shard_map/ppermute | solution.py:14
  69.1 13.2 %collective-permute-start.5 = (bf16[64,2048]{1,0:T(8,128)(2,1)S(1)}, bf16[64,2048]{1,0:T(8,128)(2,1)}, u32[]{:S(2)}, u32[]{:S(2)}) collective-permute-start(bf16[64,2048]{1,0:T(8,128)(2,1)S(1)} %convolution_convert_fusion), channel_id=1, source_target_pairs={{0,488},{8,496},{16,504},{24,0},{32,8},{40,16},{48,24},{56,32},{64... | collective-permute-start | bytes 786440 | tf_op jit(solution)/shard_map/ppermute | solution.py:14
  73.0 19.3 %all-to-all-start = ((bf16[8,8,2048]{2,1,0:T(8,128)(2,1)}), bf16[8,8,2048]{2,1,0:T(8,128)(2,1)}, u32[]{:S(2)}, u32[]{:S(2)}) async-start(bf16[8,8,2048]{2,1,0:T(8,128)(2,1)} %stack.8), calls=%async_computation | async-start | bytes 524288 | tf_op jit(solution)/shard_map/all_to_all | solution.py:162
  79.3 278.9 %all-gather.2.cloned.1.call-start = ((), (), s32[]{:S(2)}) async-start(), calls=%async_computation.1 | async-start | bytes 2359296 | tf_op jit(solution)/shard_map/all_gather | solution.py:150
  97.6 30.6 %collective-permute-start.20 = (f32[64,16,128]{2,0,1:T(8,128)S(1)}, f32[64,16,128]{2,0,1:T(8,128)}, u32[]{:S(2)}, u32[]{:S(2)}) collective-permute-start(f32[64,16,128]{2,0,1:T(8,128)S(1)} %fusion.110), channel_id=1, source_target_pairs={{0,504},{8,0},{16,8},{24,16},{32,24},{40,32},{48,40},{56,48},{64,5... | collective-permute-start | bytes 1572872 | tf_op jit(solution)/shard_map/ppermute | solution.py:14
  105.4 27.1 %collective-permute-start.21 = (f32[64,16,128]{2,0,1:T(8,128)}, f32[64,16,128]{2,0,1:T(8,128)}, u32[]{:S(2)}, u32[]{:S(2)}) collective-permute-start(f32[64,16,128]{2,0,1:T(8,128)} %fusion.109), channel_id=1, source_target_pairs={{0,8},{8,16},{16,24},{24,32},{32,40},{40,48},{48,56},{56,64},{64,7... | collective-permute-start | bytes 1572872 | tf_op jit(solution)/shard_map/ppermute | solution.py:14
  108.3 24.2 %collective-permute-start.19 = (f32[64,16,128]{2,0,1:T(8,128)}, f32[64,16,128]{2,0,1:T(8,128)}, u32[]{:S(2)}, u32[]{:S(2)}) collective-permute-start(f32[64,16,128]{2,0,1:T(8,128)} %bitcast.325), channel_id=1, source_target_pairs={{0,496},{8,504},{16,0},{24,8},{32,16},{40,24},{48,32},{56,40},{64,... | collective-permute-start | bytes 1572872 | tf_op jit(solution)/shard_map/ppermute | solution.py:14
  116.8 17.6 %collective-permute-start.22 = (f32[64,16,128]{2,0,1:T(8,128)}, f32[64,16,128]{2,0,1:T(8,128)}, u32[]{:S(2)}, u32[]{:S(2)}) collective-permute-start(f32[64,16,128]{2,0,1:T(8,128)} %bitcast.324), channel_id=1, source_target_pairs={{0,16},{8,24},{16,32},{24,40},{32,48},{40,56},{48,64},{56,72},{64,... | collective-permute-start | bytes 1572872 | tf_op jit(solution)/shard_map/ppermute | solution.py:14
  121.1 23.6 %collective-permute-start.18 = (f32[64,16,128]{2,0,1:T(8,128)}, f32[64,16,128]{2,0,1:T(8,128)}, u32[]{:S(2)}, u32[]{:S(2)}) collective-permute-start(f32[64,16,128]{2,0,1:T(8,128)} %bitcast.326), channel_id=1, source_target_pairs={{0,488},{8,496},{16,504},{24,0},{32,8},{40,16},{48,24},{56,32},{64... | collective-permute-start | bytes 1572872 | tf_op jit(solution)/shard_map/ppermute | solution.py:14
  128.2 24.1 %collective-permute-start.23 = (f32[64,16,128]{2,0,1:T(8,128)}, f32[64,16,128]{2,0,1:T(8,128)}, u32[]{:S(2)}, u32[]{:S(2)}) collective-permute-start(f32[64,16,128]{2,0,1:T(8,128)} %bitcast.323), channel_id=1, source_target_pairs={{0,24},{8,32},{16,40},{24,48},{32,56},{40,64},{48,72},{56,80},{64,... | collective-permute-start | bytes 1572872 | tf_op jit(solution)/shard_map/ppermute | solution.py:14
  360.3 18.3 %collective-permute-start.8 = (bf16[8,2048]{1,0:T(8,128)(2,1)S(1)}, bf16[8,2048]{1,0:T(8,128)(2,1)S(1)}, u32[]{:S(2)}, u32[]{:S(2)}) collective-permute-start(bf16[8,2048]{1,0:T(8,128)(2,1)S(1)} %convolution_convert_fusion.1), channel_id=1, source_target_pairs={{0,24},{8,32},{16,40},{24,48},{32,56},{40,64},{48,72},{56,80},{64,... | collective-permute-start | bytes 98312 | tf_op jit(solution)/shard_map/ppermute | solution.py:14
  362.2 21.1 %collective-permute-start.9 = (bf16[8,2048]{1,0:T(8,128)(2,1)S(1)}, bf16[8,2048]{1,0:T(8,128)(2,1)S(1)}, u32[]{:S(2)}, u32[]{:S(2)}) collective-permute-start(bf16[8,2048]{1,0:T(8,128)(2,1)S(1)} %convolution_convert_fusion.1), channel_id=1, source_target_pairs={{0,16},{8,24},{16,32},{24,40},{32,48},{40,56},{48,64},{56,72},{64,... | collective-permute-start | bytes 98312 | tf_op jit(solution)/shard_map/ppermute | solution.py:14
  364.1 19.2 %collective-permute-start.6 = (bf16[8,2048]{1,0:T(8,128)(2,1)S(1)}, bf16[8,2048]{1,0:T(8,128)(2,1)S(1)}, u32[]{:S(2)}, u32[]{:S(2)}) collective-permute-start(bf16[8,2048]{1,0:T(8,128)(2,1)S(1)} %convolution_convert_fusion.1), channel_id=1, source_target_pairs={{0,8},{8,16},{16,24},{24,32},{32,40},{40,48},{48,56},{56,64},{64,7... | collective-permute-start | bytes 98312 | tf_op jit(solution)/shard_map/ppermute | solution.py:14
  367.7 15.6 %collective-permute-start.7 = (bf16[8,2048]{1,0:T(8,128)(2,1)S(1)}, bf16[8,2048]{1,0:T(8,128)(2,1)S(1)}, u32[]{:S(2)}, u32[]{:S(2)}) collective-permute-start(bf16[8,2048]{1,0:T(8,128)(2,1)S(1)} %convolution_convert_fusion.1), channel_id=1, source_target_pairs={{0,504},{8,0},{16,8},{24,16},{32,24},{40,32},{48,40},{56,48},{64,5... | collective-permute-start | bytes 98312 | tf_op jit(solution)/shard_map/ppermute | solution.py:14
  (35 other events, 427.8 us)
Sparse Core Ops, SparseCore 0:
  92.3 75.5 all-gather.1
